TPU v7x, 32 devices: a whole 2x2x4 slice. The times are simulated.
32 devices in a mesh: ctx: 8 (over y, x, core), uly: 4 (over z).
Axes of the slice: x: 2, y: 2, z: 4, core: 2. Of those that a mesh axis runs over, the one named last changes fastest.
Arguments:
- query_states: bfloat16 [1024, 2048], P(('ctx', 'uly')), may hold values from -8 to 8
- key_states: bfloat16 [1024, 2048], P(('ctx', 'uly')), may hold values from -8 to 8
- value_states: bfloat16 [1024, 2048], P(('ctx', 'uly')), may hold values from -6 to 6
- score_kernel: float32 [16, 6, 11], P('uly'), may hold values from -0.4 to 1.2
- head_mixing: float32 [16, 4], P('uly'), may hold values from 0.25 to 1
- head_gain: float32 [2048], P('uly'), may hold values from 0.5 to 1.5
Outputs:
- attended: bfloat16 [1024, 2048], P(('ctx', 'uly'))
All inputs are finite; a program needn't handle non-finite values.
Results may differ from a plain program's by a relative error of at most 0.0049.
Values may be sent and summed in bfloat16 or wider, within the bound.
No kernel may reach another device: no remote copies, remote signals or barrier semaphores. Data moves between devices by JAX's collectives and lax.ppermute only.
A program may use at most 64 MiB of HBM per device.

v0:
```python
import jax
import jax.numpy as jnp
from jax import lax
from jax.sharding import PartitionSpec as P

GROUP = 4
QCONV = 6
KCONV = 11
lowest = -1e30
epsilon = 1e-06


def passed_along(shard, axis, by):
    peers = lax.axis_size(axis)
    pairs = [(i, i + by) for i in range(peers) if 0 <= i + by < peers]
    return lax.ppermute(shard, axis, pairs)


def partner_2(shard, axis, bit):
    return lax.ppermute(shard, axis, [(i, i ^ 1 << bit) for i in range(lax.axis_size(axis))])


def unchanged(carried):
    return carried


def group_span(shard_count, shard_rows):
    span_size = 1
    while span_size * 2 * shard_rows <= 512 and shard_count % (span_size * 2) == 0:
        span_size = span_size * 2
    return span_size


def tile_logits(query_rows, query_first, key_rows, key_first, score_kernel):
    row_lead = QCONV - 1
    col_lead = KCONV - 1
    heads = score_kernel.shape[0]
    row_count = query_rows.shape[0] - row_lead
    span_size = key_rows.shape[0]
    padded_cols = key_rows.shape[1]
    col_count = padded_cols - col_lead
    query_heads = query_rows.reshape(query_rows.shape[0], heads, -1)
    key_heads = key_rows.reshape(span_size, padded_cols, heads, -1)
    dot_scores = jnp.einsum(
        "qhd,nkhd->nhqk", query_heads, key_heads, preferred_element_type=jnp.float32
    )
    dot_scores = dot_scores * query_heads.shape[2] ** (-0.5)
    query_pos = query_first - row_lead + lax.iota(jnp.int32, query_rows.shape[0])
    key_pos = (
        key_first
        - col_lead
        + col_count * lax.iota(jnp.int32, span_size)[:, None]
        + lax.iota(jnp.int32, padded_cols)[None, :]
    )
    inside = (
        (key_pos[:, None, :] <= query_pos[None, :, None])
        & (key_pos[:, None, :] >= 0)
        & (query_pos[None, :, None] >= 0)
    )
    dot_scores = jnp.where(inside[:, None], dot_scores, 0.0)
    convolved = jnp.zeros((span_size, heads, row_count, col_count), jnp.float32)
    for row_lag in range(QCONV):
        for col_lag in range(KCONV):
            window = dot_scores[
                :,
                :,
                row_lead - row_lag : row_lead - row_lag + row_count,
                col_lead - col_lag : col_lead - col_lag + col_count,
            ]
            convolved = convolved + score_kernel[None, :, row_lag, col_lag, None, None] * window
    causal = key_pos[:, None, col_lead:] <= query_pos[None, row_lead:, None]
    return jnp.where(causal[:, None], convolved, lowest)


def stats_block(query_block, key_rows, key_first, stats_pair, score_kernel):
    query_rows, query_first = query_block
    last_query = query_first + query_rows.shape[0] - QCONV

    def stats_compute(current):
        logits = tile_logits(query_rows, query_first, key_rows, key_first, score_kernel)
        running_max, running_sum = current
        fresh_max = jnp.maximum(running_max, jnp.max(logits, axis=(0, 3)))
        rescaled = running_sum * jnp.exp(running_max - fresh_max)
        return (
            fresh_max,
            rescaled + jnp.sum(jnp.exp(logits - fresh_max[None, :, :, None]), axis=(0, 3)),
        )

    return lax.cond(key_first <= last_query, stats_compute, unchanged, stats_pair)


def output_block(
    query_block, key_rows, value_rows, key_first, weighted, stats_pair, score_kernel, head_mixing
):
    query_rows, query_first = query_block
    last_query = query_first + query_rows.shape[0] - QCONV

    def output_compute(current):
        logits = tile_logits(query_rows, query_first, key_rows, key_first, score_kernel)
        running_max, running_sum = stats_pair
        probabilities = (
            jnp.exp(logits - running_max[None, :, :, None]) / running_sum[None, :, :, None]
        )
        span_size, heads, row_count, col_count = probabilities.shape
        grouped = probabilities.reshape(span_size, heads // GROUP, GROUP, row_count, col_count)
        weights = head_mixing.reshape(heads // GROUP, GROUP, GROUP)
        mixed_probs = jnp.zeros_like(grouped)
        for source in range(GROUP):
            mixed_probs = (
                mixed_probs + weights[None, :, :, source, None, None] * grouped[:, :, source, None]
            )
        mixed_probs = mixed_probs.reshape(probabilities.shape).astype(jnp.bfloat16)
        value_heads = value_rows.reshape(span_size, col_count, heads, -1)
        return current + jnp.einsum(
            "nhqk,nkhd->qhd", mixed_probs, value_heads, preferred_element_type=jnp.float32
        )

    return lax.cond(key_first <= last_query, output_compute, unchanged, weighted)


def stats_sweep(query_blocks, key_stack, stats_all, score_kernel):
    shard_rows = key_stack.shape[1] - (KCONV - 1)
    span_size = group_span(key_stack.shape[0], shard_rows)
    spans = key_stack.reshape((key_stack.shape[0] // span_size, span_size) + key_stack.shape[1:])

    def stats_advance(step_index, carried):
        key_rows = lax.dynamic_index_in_dim(spans, step_index, 0, keepdims=False)
        key_first = step_index * span_size * shard_rows
        return tuple(
            (
                stats_block(query_block, key_rows, key_first, stats_pair, score_kernel)
                for query_block, stats_pair in zip(query_blocks, carried)
            )
        )

    return lax.fori_loop(0, spans.shape[0], stats_advance, stats_all)


def output_sweep(
    query_blocks, key_stack, value_stack, weighted_all, stats_all, score_kernel, head_mixing
):
    shard_rows = value_stack.shape[1]
    span_size = group_span(key_stack.shape[0], shard_rows)
    key_spans = key_stack.reshape(
        (key_stack.shape[0] // span_size, span_size) + key_stack.shape[1:]
    )
    value_spans = value_stack.reshape(
        (value_stack.shape[0] // span_size, span_size) + value_stack.shape[1:]
    )

    def output_advance(step_index, carried):
        key_rows = lax.dynamic_index_in_dim(key_spans, step_index, 0, keepdims=False)
        value_rows = lax.dynamic_index_in_dim(value_spans, step_index, 0, keepdims=False)
        key_first = step_index * span_size * shard_rows
        return tuple(
            (
                output_block(
                    query_block,
                    key_rows,
                    value_rows,
                    key_first,
                    weighted,
                    stats_pair,
                    score_kernel,
                    head_mixing,
                )
                for query_block, weighted, stats_pair in zip(query_blocks, carried, stats_all)
            )
        )

    return lax.fori_loop(0, key_spans.shape[0], output_advance, weighted_all)


def normalize(weighted, gain_local):
    factor = lax.rsqrt(jnp.mean(weighted * weighted, axis=2, keepdims=True) + epsilon)
    return (
        (weighted * factor * gain_local[None]).astype(jnp.bfloat16).reshape(weighted.shape[0], -1)
    )


def shards(query_states, key_states, value_states, score_kernel, head_mixing, head_gain):
    query_local, key_local, value_local = (
        lax.all_to_all(query_states, "uly", split_axis=1, concat_axis=0, tiled=True),
        lax.all_to_all(key_states, "uly", split_axis=1, concat_axis=0, tiled=True),
        lax.all_to_all(value_states, "uly", split_axis=1, concat_axis=0, tiled=True),
    )
    shard_rows = query_local.shape[0]
    row_lead = QCONV - 1
    col_lead = KCONV - 1
    heads = score_kernel.shape[0]
    head_dim = query_local.shape[1] // heads
    ctx_count = lax.axis_size("ctx")
    ctx_place = lax.axis_index("ctx")
    tails = jnp.concatenate(
        [query_local[shard_rows - row_lead :], key_local[shard_rows - col_lead :]], axis=0
    )
    earlier = passed_along(tails, "ctx", 1)
    query_ext = jnp.concatenate([earlier[:row_lead], query_local], axis=0)
    key_ext = jnp.concatenate([earlier[row_lead:], key_local], axis=0)
    query_first = ctx_place * shard_rows
    half_rows = shard_rows // 2
    top_bit = ctx_count.bit_length() - 2
    far_rows = partner_2(query_ext[half_rows:], "ctx", top_bit)
    partner = jnp.where(
        ctx_place < ctx_count // 2, ctx_place + ctx_count // 2, ctx_place - ctx_count // 2
    )
    query_blocks = [
        (query_ext[: half_rows + row_lead], query_first),
        (far_rows, partner * shard_rows + half_rows),
    ]
    stats_all = tuple(
        (
            (
                jnp.full((heads, block_rows.shape[0] - row_lead), lowest, jnp.float32),
                jnp.zeros((heads, block_rows.shape[0] - row_lead), jnp.float32),
            )
            for block_rows, block_first in query_blocks
        )
    )
    weighted_all = tuple(
        (
            jnp.zeros((block_rows.shape[0] - row_lead, heads, head_dim), jnp.float32)
            for block_rows, block_first in query_blocks
        )
    )
    key_stack = key_ext[None]
    value_stack = value_local[None]
    stats_all = stats_sweep(
        query_blocks, lax.all_gather(key_stack, "ctx", axis=0, tiled=True), stats_all, score_kernel
    )
    weighted_all = output_sweep(
        query_blocks,
        lax.all_gather(key_stack, "ctx", axis=0, tiled=True),
        lax.all_gather(value_stack, "ctx", axis=0, tiled=True),
        weighted_all,
        stats_all,
        score_kernel,
        head_mixing,
    )
    gain_local = head_gain.reshape(heads, head_dim)
    finished = [normalize(weighted, gain_local) for weighted in weighted_all]
    returned = partner_2(finished[1], "ctx", top_bit)
    attended = jnp.concatenate([finished[0], returned], axis=0)
    return lax.all_to_all(attended, "uly", split_axis=0, concat_axis=1, tiled=True)


def solution(mesh):
    placed = (
        P(("ctx", "uly"), None),
        P(("ctx", "uly"), None),
        P(("ctx", "uly"), None),
        P("uly", None, None),
        P("uly", None),
        P("uly"),
    )
    return jax.shard_map(
        shards, mesh=mesh, in_specs=placed, out_specs=P(("ctx", "uly"), None), check_vma=False
    )
```

profile of v0, /device:TPU:0, one launch (start us, length us, event | category | flops | bytes accessed | tf_op | source)
XLA Modules:
  0.0 152.9 jit_solution(973212687336004941)
XLA Ops:
  6.5 1.6 %copy.144 = bf16[4,4,8,512]{3,2,0,1:T(8,128)(2,1)} copy(bf16[4,4,8,512]{3,2,1,0:T(8,128)(2,1)} %bitcast.667) | data formatting | bytes 262144 | tf_op jit(solution)/shard_map/all_to_all | solution.py:184
  8.1 6.4 %all-to-all-start.1 = ((bf16[32,4,512]{2,0,1:T(8,128)(2,1)}), bf16[32,4,512]{2,0,1:T(8,128)(2,1)S(1)}, u32[]{:S(2)}, u32[]{:S(2)}) async-start(bf16[32,4,512]{2,0,1:T(8,128)(2,1)} %bitcast.640), calls=%async_computation.1 | async-start | bytes 262144 | tf_op jit(solution)/shard_map/all_to_all | solution.py:184
  14.6 1.6 %copy.145 = bf16[4,4,8,512]{3,2,0,1:T(8,128)(2,1)} copy(bf16[4,4,8,512]{3,2,1,0:T(8,128)(2,1)} %bitcast.668) | data formatting | bytes 262144 | tf_op jit(solution)/shard_map/all_to_all | solution.py:183
  16.2 4.5 %all-to-all-done.1 = bf16[32,4,512]{2,0,1:T(8,128)(2,1)S(1)} async-done(((bf16[32,4,512]{2,0,1:T(8,128)(2,1)}), bf16[32,4,512]{2,0,1:T(8,128)(2,1)S(1)}, u32[]{:S(2)}, u32[]{:S(2)}) %all-to-all-start.1) | async-done | bytes 131104 | tf_op jit(solution)/shard_map/all_to_all | solution.py:184
  20.7 3.3 %all-to-all-start = ((bf16[32,4,512]{2,0,1:T(8,128)(2,1)}), bf16[32,4,512]{2,0,1:T(8,128)(2,1)S(1)}, u32[]{:S(2)}, u32[]{:S(2)}) async-start(bf16[32,4,512]{2,0,1:T(8,128)(2,1)} %bitcast.641), calls=%async_computation | async-start | bytes 262144 | tf_op jit(solution)/shard_map/all_to_all | solution.py:183
  24.1 5.8 %all-to-all-done = bf16[32,4,512]{2,0,1:T(8,128)(2,1)S(1)} async-done(((bf16[32,4,512]{2,0,1:T(8,128)(2,1)}), bf16[32,4,512]{2,0,1:T(8,128)(2,1)S(1)}, u32[]{:S(2)}, u32[]{:S(2)}) %all-to-all-start) | async-done | bytes 131104 | tf_op jit(solution)/shard_map/all_to_all | solution.py:183
  29.9 1.3 collective-permute-start
  32.8 9.0 %all_to_all.73 = bf16[32,4,512]{2,0,1:T(8,128)(2,1)} all-to-all(bf16[32,4,512]{2,0,1:T(8,128)(2,1)S(1)} %bitcast.665), channel_id=1, replica_groups=mesh['ctx'=8,'uly'=4] {'uly'}, dimensions={1} | all-to-all | bytes 262144 | tf_op jit(solution)/shard_map/all_to_all | solution.py:185
  41.9 5.4 %collective-permute-start.1 = (bf16[69,512]{1,0:T(8,128)(2,1)S(1)}, bf16[69,512]{1,0:T(8,128)(2,1)S(1)}, u32[]{:S(2)}, u32[]{:S(2)}) collective-permute-start(bf16[69,512]{1,0:T(8,128)(2,1)S(1)} %get-tuple-element.1401), channel_id=1, source_target_pairs={{0,16},{4,20},{8,24},{12,28},{16,0},{20,4},{24,8},{28,12},{1,17},{... | collective-permute-start | bytes 211976 | tf_op jit(solution)/shard_map/ppermute | solution.py:20
  47.4 2.2 %collective-permute-done.1 = bf16[69,512]{1,0:T(8,128)(2,1)S(1)} collective-permute-done((bf16[69,512]{1,0:T(8,128)(2,1)S(1)}, bf16[69,512]{1,0:T(8,128)(2,1)S(1)}, u32[]{:S(2)}, u32[]{:S(2)}) %collective-permute-start.1) | collective-permute-done | bytes 70688 | tf_op jit(solution)/shard_map/ppermute | solution.py:20
  49.6 9.5 %all-gather.7.cloned.1.call-done = bf16[8,138,512]{2,1,0:T(8,128)(2,1)} async-done(((bf16[1,138,512]{2,1,0:T(8,128)(2,1)}), bf16[8,138,512]{2,1,0:T(8,128)(2,1)}) %all-gather.7.cloned.1.call-update) | async-done | bytes 1130512 | tf_op jit(solution)/shard_map/all_gather | solution.py:233
  59.1 34.9 %while.46 = (s32[]{:T(128)}, f32[4,64]{1,0:T(4,128)S(1)}, f32[4,64]{1,0:T(4,128)S(1)}, f32[4,64]{1,0:T(4,128)S(1)}, f32[4,64]{1,0:T(4,128)S(1)}, /*index=5*/s32[...) while((s32[]{:T(128)}, f32[4,64]{1,0:T(4,128)S(1)}, ...), condition=%wide.region_9.10_spmd, body=%wide.region_0.9_spmd.sunk | while | flops 114301904 | bytes 77811088 | solution.py:136
  59.1 1.1 dynamic-slice_bitcast_fusion.6
  60.2 10.9 %conditional.8 = ((f32[4,64]{1,0:T(4,128)S(1)}, f32[4,64]{1,0:T(4,128)S(1)})) conditional(s32[]{:T(128)} %convert_element_type.72, (f32[4,64]{1,0:T(4,128)S(1)}, f32[4,64]{1,0:T(4,128)S(1)}) %tuple.395, (s32[]{:T(128)}, s32[]{:T(128)}, f32[4,6,11]{0,2,1:T(8,128)S(1)}, bf16[4,138,512]{2,1,0:T(8,128)(2,1)S(1)}, bf16[69,512]{1,0:T(8,128)(2,1)S(1)}, ...), branch_computations={%region_1.1_spmd, %region_2.4_spmd} | conditional | flops 57150952 | bytes 38340128 | solution.py:89
  61.7 9.2 %fusion.312 = (f32[4,64]{1,0:T(4,128)S(1)}, f32[4,4,64,128]{3,2,0,1:T(8,128)S(1)}) fusion(f32[4,4,69,138]{3,2,0,1:T(8,128)S(1)} %fusion.1, f32[4]{0:T(128)S(1)} %get-tuple-element.1270, f32[4]{0:T(128)S(1)} %get-tuple-element.1271, f32[4]{0:T(128)S(1)} %get-tuple-element.1272, f32[4]{0:T(128)S(1)} %get-tuple-element.1273, f32[4]{0:T(128)S(1)} %get-tuple-element.1274, ...), kind=kLoop, calls=%fused_computation.914 | loop fusion | flops 17432320 | bytes 35162144 | tf_op jit(solution)/shard_map/while/body/eval_jaxpr/cond/branch_1_fun/reduce_max | solution.py:82
  71.1 10.9 %conditional.9 = ((f32[4,64]{1,0:T(4,128)S(1)}, f32[4,64]{1,0:T(4,128)S(1)})) conditional(s32[]{:T(128)} %convert_element_type.73, (f32[4,64]{1,0:T(4,128)S(1)}, f32[4,64]{1,0:T(4,128)S(1)}) %tuple.397, (s32[]{:T(128)}, s32[]{:T(128)}, f32[4,6,11]{0,2,1:T(8,128)S(1)}, bf16[4,138,512]{2,1,0:T(8,128)(2,1)S(1)}, bf16[69,512]{1,0:T(8,128)(2,1)S(1)}, ...), branch_computations={%region_5.5_spmd, %region_6.8_spmd} | conditional | flops 57150952 | bytes 38340128 | solution.py:89
  72.5 9.2 %fusion.314 = (f32[4,64]{1,0:T(4,128)S(1)}, f32[4,4,64,128]{3,2,0,1:T(8,128)S(1)}) fusion(f32[4,4,69,138]{3,2,0,1:T(8,128)S(1)} %fusion.71, f32[4]{0:T(128)S(1)} %get-tuple-element.1336, f32[4]{0:T(128)S(1)} %get-tuple-element.1337, f32[4]{0:T(128)S(1)} %get-tuple-element.1338, f32[4]{0:T(128)S(1)} %get-tuple-element.1339, f32[4]{0:T(128)S(1)} %get-tuple-element.1340, ...), kind=kLoop, calls=%fused_computation.915 | loop fusion | flops 17432320 | bytes 35162144 | tf_op jit(solution)/shard_map/while/body/eval_jaxpr/cond/branch_1_fun/reduce_max | solution.py:82
  82.0 1.1 dynamic-slice_bitcast_fusion.6
  83.2 10.9 %conditional.9 = ((f32[4,64]{1,0:T(4,128)S(1)}, f32[4,64]{1,0:T(4,128)S(1)})) conditional(s32[]{:T(128)} %convert_element_type.73, (f32[4,64]{1,0:T(4,128)S(1)}, f32[4,64]{1,0:T(4,128)S(1)}) %tuple.397, (s32[]{:T(128)}, s32[]{:T(128)}, f32[4,6,11]{0,2,1:T(8,128)S(1)}, bf16[4,138,512]{2,1,0:T(8,128)(2,1)S(1)}, bf16[69,512]{1,0:T(8,128)(2,1)S(1)}, ...), branch_computations={%region_5.5_spmd, %region_6.8_spmd} | conditional | flops 57150952 | bytes 38340128 | solution.py:89
  84.6 9.2 %fusion.314 = (f32[4,64]{1,0:T(4,128)S(1)}, f32[4,4,64,128]{3,2,0,1:T(8,128)S(1)}) fusion(f32[4,4,69,138]{3,2,0,1:T(8,128)S(1)} %fusion.71, f32[4]{0:T(128)S(1)} %get-tuple-element.1336, f32[4]{0:T(128)S(1)} %get-tuple-element.1337, f32[4]{0:T(128)S(1)} %get-tuple-element.1338, f32[4]{0:T(128)S(1)} %get-tuple-element.1339, f32[4]{0:T(128)S(1)} %get-tuple-element.1340, ...), kind=kLoop, calls=%fused_computation.915 | loop fusion | flops 17432320 | bytes 35162144 | tf_op jit(solution)/shard_map/while/body/eval_jaxpr/cond/branch_1_fun/reduce_max | solution.py:82
  94.1 36.3 %while.47 = (s32[]{:T(128)}, f32[64,4,128]{2,0,1:T(8,128)S(1)}, f32[64,4,128]{2,0,1:T(8,128)S(1)}, s32[]{:T(128)}, bf16[2,4,138,512]{3,2,1,0:T(8,128)(2,1)}, /*i...) while((s32[]{:T(128)}, f32[64,4,128]{2,0,1:T(8,128)S(1)}, ...), condition=%wide.region_15.16_spmd, body=%wide.region_10.15_spmd.sunk | while | flops 183310304 | bytes 86701888 | solution.py:171
  94.3 1.2 dynamic-slice_bitcast_fusion.7
  95.8 11.1 %conditional.10 = (f32[64,4,128]{2,0,1:T(8,128)S(1)}) conditional(s32[]{:T(128)} %convert_element_type.74, f32[64,4,128]{2,0,1:T(8,128)S(1)} %get-tuple-element.1670, (f32[4,4]{1,0:T(4,128)S(1)}, s32[]{:T(128)}, s32[]{:T(128)}, f32[4,6,11]{0,2,1:T(8,128)S(1)}, bf16[4,138,512]{2,1,0:T(8,128)(2,1)S(1)}, /*index=5*/bf16[69,512]{1,0:T(8,128)(2,1)S(1)}, ...), branch_computations={%region_11.11_spmd, %region_12.12_spmd} | conditional | flops 91655144 | bytes 40164048 | solution.py:118
  97.2 9.0 %fusion.151 = f32[4,1,4,64,128]{4,3,0,2,1:T(8,128)S(1)} fusion(f32[4,4,69,138]{3,2,0,1:T(8,128)S(1)} %fusion.141, f32[4,64]{1,0:T(4,128)S(1)} %get-tuple-element.865, f32[4,64]{1,0:T(4,128)S(1)} %get-tuple-element.864, f32[4]{0:T(128)S(1)} %get-tuple-element.1134, f32[4]{0:T(128)S(1)} %get-tuple-element.1135, f32[4]{0:T(128)S(1)} %get-tuple-element.1136, ...), kind=kLoop, calls=%fused_computation.439 | loop fusion | flops 17563648 | bytes 35163168 | tf_op jit(solution)/shard_map/while/body/eval_jaxpr/cond/branch_1_fun/reshape | solution.py:105
  106.8 11.0 %conditional.11 = (f32[64,4,128]{2,0,1:T(8,128)S(1)}) conditional(s32[]{:T(128)} %convert_element_type.75, f32[64,4,128]{2,0,1:T(8,128)S(1)} %get-tuple-element.1671, (f32[4,4]{1,0:T(4,128)S(1)}, s32[]{:T(128)}, s32[]{:T(128)}, f32[4,6,11]{0,2,1:T(8,128)S(1)}, bf16[4,138,512]{2,1,0:T(8,128)(2,1)S(1)}, /*index=5*/bf16[69,512]{1,0:T(8,128)(2,1)S(1)}, ...), branch_computations={%region_13.13_spmd, %region_14.14_spmd} | conditional | flops 91655144 | bytes 40164048 | solution.py:118
  108.2 9.0 %fusion.236 = f32[4,1,4,64,128]{4,3,0,2,1:T(8,128)S(1)} fusion(f32[4,4,69,138]{3,2,0,1:T(8,128)S(1)} %fusion.226, f32[4,64]{1,0:T(4,128)S(1)} %get-tuple-element.875, f32[4,64]{1,0:T(4,128)S(1)} %get-tuple-element.874, f32[4]{0:T(128)S(1)} %get-tuple-element.1204, f32[4]{0:T(128)S(1)} %get-tuple-element.1205, f32[4]{0:T(128)S(1)} %get-tuple-element.1206, ...), kind=kLoop, calls=%fused_computation.674 | loop fusion | flops 17563648 | bytes 35163168 | tf_op jit(solution)/shard_map/while/body/eval_jaxpr/cond/branch_1_fun/reshape | solution.py:105
  117.9 1.2 dynamic-slice_bitcast_fusion.7
  119.4 11.0 %conditional.11 = (f32[64,4,128]{2,0,1:T(8,128)S(1)}) conditional(s32[]{:T(128)} %convert_element_type.75, f32[64,4,128]{2,0,1:T(8,128)S(1)} %get-tuple-element.1671, (f32[4,4]{1,0:T(4,128)S(1)}, s32[]{:T(128)}, s32[]{:T(128)}, f32[4,6,11]{0,2,1:T(8,128)S(1)}, bf16[4,138,512]{2,1,0:T(8,128)(2,1)S(1)}, /*index=5*/bf16[69,512]{1,0:T(8,128)(2,1)S(1)}, ...), branch_computations={%region_13.13_spmd, %region_14.14_spmd} | conditional | flops 91655144 | bytes 40164048 | solution.py:118
  120.8 9.0 %fusion.236 = f32[4,1,4,64,128]{4,3,0,2,1:T(8,128)S(1)} fusion(f32[4,4,69,138]{3,2,0,1:T(8,128)S(1)} %fusion.226, f32[4,64]{1,0:T(4,128)S(1)} %get-tuple-element.875, f32[4,64]{1,0:T(4,128)S(1)} %get-tuple-element.874, f32[4]{0:T(128)S(1)} %get-tuple-element.1204, f32[4]{0:T(128)S(1)} %get-tuple-element.1205, f32[4]{0:T(128)S(1)} %get-tuple-element.1206, ...), kind=kLoop, calls=%fused_computation.674 | loop fusion | flops 17563648 | bytes 35163168 | tf_op jit(solution)/shard_map/while/body/eval_jaxpr/cond/branch_1_fun/reshape | solution.py:105
  130.8 1.5 collective-permute-start.2
  132.3 2.8 %collective-permute-done.2 = bf16[64,512]{1,0:T(8,128)(2,1)S(1)} collective-permute-done((bf16[64,512]{1,0:T(8,128)(2,1)S(1)}, bf16[64,512]{1,0:T(8,128)(2,1)S(1)}, u32[]{:S(2)}, u32[]{:S(2)}) %collective-permute-start.2) | collective-permute-done | bytes 65568 | tf_op jit(solution)/shard_map/ppermute | solution.py:20
  135.1 10.3 %all_to_all.74 = bf16[4,32,512]{2,1,0:T(8,128)(2,1)S(1)} all-to-all(bf16[4,32,512]{2,1,0:T(8,128)(2,1)S(1)} %bitcast.663), channel_id=1, replica_groups=mesh['ctx'=8,'uly'=4] {'uly'}, dimensions={0} | all-to-all | bytes 262144 | tf_op jit(solution)/shard_map/all_to_all | solution.py:244
  (162 shorter events, 13.9 us)
Async XLA Ops:
  6.5 26.3 %copy-start.2 = (bf16[32,2048]{1,0:T(8,128)(2,1)S(1)}, bf16[32,2048]{1,0:T(8,128)(2,1)}, u32[]{:S(2)}) copy-start(bf16[32,2048]{1,0:T(8,128)(2,1)} %param.20) | copy-start | bytes 393220
  8.1 39.2 %copy-start.3 = (f32[4,6,11]{2,0,1:T(4,128)S(1)}, f32[4,6,11]{2,0,1:T(4,128)}, u32[]{:S(2)}) copy-start(f32[4,6,11]{2,0,1:T(4,128)} %param.21) | copy-start | bytes 3172
  8.1 12.5 %all-to-all-start.1 = ((bf16[32,4,512]{2,0,1:T(8,128)(2,1)}), bf16[32,4,512]{2,0,1:T(8,128)(2,1)S(1)}, u32[]{:S(2)}, u32[]{:S(2)}) async-start(bf16[32,4,512]{2,0,1:T(8,128)(2,1)} %bitcast.640), calls=%async_computation.1 | async-start | bytes 262144 | tf_op jit(solution)/shard_map/all_to_all | solution.py:184
  20.7 9.2 %all-to-all-start = ((bf16[32,4,512]{2,0,1:T(8,128)(2,1)}), bf16[32,4,512]{2,0,1:T(8,128)(2,1)S(1)}, u32[]{:S(2)}, u32[]{:S(2)}) async-start(bf16[32,4,512]{2,0,1:T(8,128)(2,1)} %bitcast.641), calls=%async_computation | async-start | bytes 262144 | tf_op jit(solution)/shard_map/all_to_all | solution.py:183
  24.0 35.1 %all-gather.7.cloned.1.call-start = ((), (), s32[]{:S(2)}) async-start(), calls=%async_computation.5 | async-start | bytes 1327104 | tf_op jit(solution)/shard_map/all_gather | solution.py:233
  29.9 2.1 %collective-permute-start = (bf16[15,512]{1,0:T(8,128)(2,1)S(1)}, bf16[15,512]{1,0:T(8,128)(2,1)S(1)}, u32[]{:S(2)}, u32[]{:S(2)}) collective-permute-start(bf16[15,512]{1,0:T(8,128)(2,1)S(1)} %pad_maximum_fusion.2), channel_id=1, source_target_pairs={{0,4},{4,8},{8,12},{12,16},{16,20},{20,24},{24,28},{1,5},{5,9},{9,... | collective-permute-start | bytes 46088 | tf_op jit(solution)/shard_map/ppermute | solution.py:16
  32.8 61.3 %all-gather.5.cloned.1.call-start = ((), (), s32[]{:S(2)}) async-start(), calls=%async_computation.4 | async-start | bytes 1179648 | tf_op jit(solution)/shard_map/all_gather | solution.py:234
  41.9 7.7 %collective-permute-start.1 = (bf16[69,512]{1,0:T(8,128)(2,1)S(1)}, bf16[69,512]{1,0:T(8,128)(2,1)S(1)}, u32[]{:S(2)}, u32[]{:S(2)}) collective-permute-start(bf16[69,512]{1,0:T(8,128)(2,1)S(1)} %get-tuple-element.1401), channel_id=1, source_target_pairs={{0,16},{4,20},{8,24},{12,28},{16,0},{20,4},{24,8},{28,12},{1,17},{... | collective-permute-start | bytes 211976 | tf_op jit(solution)/shard_map/ppermute | solution.py:20
  59.1 35.0 %copy-start.1 = (f32[4,4]{1,0:T(4,128)S(1)}, f32[4,4]{1,0:T(4,128)}, u32[]{:S(2)}) copy-start(f32[4,4]{1,0:T(4,128)} %param.22) | copy-start | bytes 196
  94.1 36.5 %copy-start.4 = (f32[512]{0:T(512)S(1)}, f32[512]{0:T(512)}, u32[]{:S(2)}) copy-start(f32[512]{0:T(512)} %param.23) | copy-start | bytes 6148
  94.3 1.4 copy-start
  117.9 1.4 copy-start
  130.8 4.3 %collective-permute-start.2 = (bf16[64,512]{1,0:T(8,128)(2,1)S(1)}, bf16[64,512]{1,0:T(8,128)(2,1)S(1)}, u32[]{:S(2)}, u32[]{:S(2)}) collective-permute-start(bf16[64,512]{1,0:T(8,128)(2,1)S(1)} %bitcast.670), channel_id=1, source_target_pairs={{0,16},{4,20},{8,24},{12,28},{16,0},{20,4},{24,8},{28,12},{1,17},{... | collective-permute-start | bytes 196616 | tf_op jit(solution)/shard_map/ppermute | solution.py:20
Sparse Core Ops, SparseCore 0:
  32.9 26.1 all-gather.6
  61.0 23.6 all-gather.4
where the time goes:
time: 154 us; the launch traced here: 153 us
  other arithmetic  58.6 us (38%)
  waiting for transfers between devices  25.7 us (17%)
  blocking collectives  19.3 us (13%)
  starting transfers between devices  18 us (12%)
  between operations  13.6 us (9%)
  local copies, waits for them, and re-layouts  12.4 us (8%)
  matrix products  4.27 us (3%)
    reduce_max x3, other arithmetic, stats_compute(): fresh_max = jnp.maximum(running_max, jnp.max(logits, axis=(0, 3)))  27.5 us
    reshape x3, other arithmetic, output_compute(): probabilities.reshape(span_size, heads // GROUP, GROUP, row_count, col_co...  27 us
    all_to_all x1, blocking collectives, shards(): lax.all_to_all(attended, 'uly', split_axis=0, concat_axis=1, tiled=True)  10.3 us
    all_gather x1, waiting for transfers between devices, shards(): lax.all_gather(key_stack, 'ctx', axis=0, tiled=True)  9.46 us
    all_to_all x1, blocking collectives, shards(): lax.all_to_all(value_states, 'uly', split_axis=1, concat_axis=0, tiled=True)  9.01 us
    ppermute x2, starting transfers between devices, partner_2(): lax.ppermute(shard, axis, [(i, i ^ 1 << bit) for i in range(lax.axis_size...  6.88 us
    all_to_all x1, starting transfers between devices, shards(): lax.all_to_all(key_states, 'uly', split_axis=1, concat_axis=0, tiled=True)  6.45 us
    all_to_all x1, waiting for transfers between devices, shards(): lax.all_to_all(query_states, 'uly', split_axis=1, concat_axis=0, tiled=True)  5.82 us
  transfers between devices with their start and end apart: 7, of which 6 were waited for; matrix products, arithmetic and copies ran while one was open for 24% of the time, Pallas kernels for 0%

commit v1 on v0

--- a/solution.py
+++ b/solution.py
@@ -181,7 +181,12 @@
 def shards(query_states, key_states, value_states, score_kernel, head_mixing, head_gain):
     query_local, key_local, value_local = (
         lax.all_to_all(query_states, "uly", split_axis=1, concat_axis=0, tiled=True),
-        lax.all_to_all(key_states, "uly", split_axis=1, concat_axis=0, tiled=True),
+        jnp.concatenate(
+            lax.all_to_all(
+                jnp.stack(jnp.split(key_states, lax.axis_size("uly"), axis=1)), "uly", 0, 0
+            ),
+            axis=0,
+        ),
         lax.all_to_all(value_states, "uly", split_axis=1, concat_axis=0, tiled=True),
     )
     shard_rows = query_local.shape[0]

time: 154 us -> 153 us (level)
    all_to_all x1 -> x0, local copies, waits for them, and re-layouts: 1.6 us -> none  [shards(): lax.all_to_all(key_states, 'uly', split_axis=1, concat_axis=0, tiled=True)]
where the time goes in v1:
time: 153 us
  other arithmetic  59.3 us (39%)
  waiting for transfers between devices  25.7 us (17%)
  blocking collectives  19.3 us (13%)
  starting transfers between devices  18 us (12%)
  between operations  13.6 us (9%)
  local copies, waits for them, and re-layouts  11.6 us (8%)
  matrix products  4.26 us (3%)
    reduce_max x3, other arithmetic, stats_compute(): fresh_max = jnp.maximum(running_max, jnp.max(logits, axis=(0, 3)))  27.5 us
    reshape x3, other arithmetic, output_compute(): probabilities.reshape(span_size, heads // GROUP, GROUP, row_count, col_co...  27 us
    all_to_all x1, blocking collectives, shards(): lax.all_to_all(attended, 'uly', split_axis=0, concat_axis=1, tiled=True)  10.3 us
    all_gather x1, waiting for transfers between devices, shards(): lax.all_gather(key_stack, 'ctx', axis=0, tiled=True)  9.46 us
    all_to_all x1, blocking collectives, shards(): lax.all_to_all(value_states, 'uly', split_axis=1, concat_axis=0, tiled=True)  9 us
    ppermute x2, starting transfers between devices, partner_2(): lax.ppermute(shard, axis, [(i, i ^ 1 << bit) for i in range(lax.axis_size...  6.88 us
    all_to_all x1, starting transfers between devices, shards(): lax.all_to_all(jnp.stack(jnp.split(key_states, lax.axis_size('uly'), axis...  6.45 us
    all_to_all x1, waiting for transfers between devices, shards(): lax.all_to_all(query_states, 'uly', split_axis=1, concat_axis=0, tiled=True)  5.82 us
  transfers between devices with their start and end apart: 7, of which 6 were waited for; matrix products, arithmetic and copies ran while one was open for 24% of the time, Pallas kernels for 0%

profile of v1, /device:TPU:0, one launch (start us, length us, event | category | flops | bytes accessed | tf_op | source)
XLA Modules:
  0.0 152.9 jit_solution(4188716929185169899)
XLA Ops:
  6.5 0.9 slice_bitcast_fusion.275
  8.1 6.4 %all-to-all-start.1 = ((bf16[4,32,512]{2,1,0:T(8,128)(2,1)}), bf16[4,32,512]{2,1,0:T(8,128)(2,1)S(1)}, u32[]{:S(2)}, u32[]{:S(2)}) async-start(bf16[4,32,512]{2,1,0:T(8,128)(2,1)} %pad_maximum_fusion), calls=%async_computation.1 | async-start | bytes 262144 | tf_op jit(solution)/shard_map/all_to_all | solution.py:185
  14.5 1.6 %copy.137 = bf16[4,4,8,512]{3,2,0,1:T(8,128)(2,1)} copy(bf16[4,4,8,512]{3,2,1,0:T(8,128)(2,1)} %bitcast.669) | data formatting | bytes 262144 | tf_op jit(solution)/shard_map/all_to_all | solution.py:183
  16.1 4.5 %all-to-all-done.1 = bf16[4,32,512]{2,1,0:T(8,128)(2,1)S(1)} async-done(((bf16[4,32,512]{2,1,0:T(8,128)(2,1)}), bf16[4,32,512]{2,1,0:T(8,128)(2,1)S(1)}, u32[]{:S(2)}, u32[]{:S(2)}) %all-to-all-start.1) | async-done | bytes 131104 | tf_op jit(solution)/shard_map/all_to_all | solution.py:185
  20.6 3.3 %all-to-all-start = ((bf16[32,4,512]{2,0,1:T(8,128)(2,1)}), bf16[32,4,512]{2,0,1:T(8,128)(2,1)S(1)}, u32[]{:S(2)}, u32[]{:S(2)}) async-start(bf16[32,4,512]{2,0,1:T(8,128)(2,1)} %bitcast.643), calls=%async_computation | async-start | bytes 262144 | tf_op jit(solution)/shard_map/all_to_all | solution.py:183
  24.0 5.8 %all-to-all-done = bf16[32,4,512]{2,0,1:T(8,128)(2,1)S(1)} async-done(((bf16[32,4,512]{2,0,1:T(8,128)(2,1)}), bf16[32,4,512]{2,0,1:T(8,128)(2,1)S(1)}, u32[]{:S(2)}, u32[]{:S(2)}) %all-to-all-start) | async-done | bytes 131104 | tf_op jit(solution)/shard_map/all_to_all | solution.py:183
  29.8 1.3 collective-permute-start
  32.8 9.0 %all_to_all.59 = bf16[32,4,512]{2,0,1:T(8,128)(2,1)} all-to-all(bf16[32,4,512]{2,0,1:T(8,128)(2,1)S(1)} %bitcast.667), channel_id=1, replica_groups=mesh['ctx'=8,'uly'=4] {'uly'}, dimensions={1} | all-to-all | bytes 262144 | tf_op jit(solution)/shard_map/all_to_all | solution.py:190
  41.8 5.4 %collective-permute-start.1 = (bf16[69,512]{1,0:T(8,128)(2,1)S(1)}, bf16[69,512]{1,0:T(8,128)(2,1)S(1)}, u32[]{:S(2)}, u32[]{:S(2)}) collective-permute-start(bf16[69,512]{1,0:T(8,128)(2,1)S(1)} %get-tuple-element.1401), channel_id=1, source_target_pairs={{0,16},{4,20},{8,24},{12,28},{16,0},{20,4},{24,8},{28,12},{1,17},{... | collective-permute-start | bytes 211976 | tf_op jit(solution)/shard_map/ppermute | solution.py:20
  47.3 2.2 %collective-permute-done.1 = bf16[69,512]{1,0:T(8,128)(2,1)S(1)} collective-permute-done((bf16[69,512]{1,0:T(8,128)(2,1)S(1)}, bf16[69,512]{1,0:T(8,128)(2,1)S(1)}, u32[]{:S(2)}, u32[]{:S(2)}) %collective-permute-start.1) | collective-permute-done | bytes 70688 | tf_op jit(solution)/shard_map/ppermute | solution.py:20
  49.6 9.5 %all-gather.7.cloned.1.call-done = bf16[8,138,512]{2,1,0:T(8,128)(2,1)} async-done(((bf16[1,138,512]{2,1,0:T(8,128)(2,1)}), bf16[8,138,512]{2,1,0:T(8,128)(2,1)}) %all-gather.7.cloned.1.call-update) | async-done | bytes 1130512 | tf_op jit(solution)/shard_map/all_gather | solution.py:238
  59.0 34.9 %while.46 = (s32[]{:T(128)}, f32[4,64]{1,0:T(4,128)S(1)}, f32[4,64]{1,0:T(4,128)S(1)}, f32[4,64]{1,0:T(4,128)S(1)}, f32[4,64]{1,0:T(4,128)S(1)}, /*index=5*/s32[...) while((s32[]{:T(128)}, f32[4,64]{1,0:T(4,128)S(1)}, ...), condition=%wide.region_9.10_spmd, body=%wide.region_0.9_spmd.sunk | while | flops 114301904 | bytes 77811088 | solution.py:136
  59.1 1.1 dynamic-slice_bitcast_fusion.6
  60.2 10.9 %conditional.8 = ((f32[4,64]{1,0:T(4,128)S(1)}, f32[4,64]{1,0:T(4,128)S(1)})) conditional(s32[]{:T(128)} %convert_element_type.72, (f32[4,64]{1,0:T(4,128)S(1)}, f32[4,64]{1,0:T(4,128)S(1)}) %tuple.398, (s32[]{:T(128)}, s32[]{:T(128)}, f32[4,6,11]{0,2,1:T(8,128)S(1)}, bf16[4,138,512]{2,1,0:T(8,128)(2,1)S(1)}, bf16[69,512]{1,0:T(8,128)(2,1)S(1)}, ...), branch_computations={%region_1.1_spmd, %region_2.4_spmd} | conditional | flops 57150952 | bytes 38340128 | solution.py:89
  61.6 9.2 %fusion.312 = (f32[4,64]{1,0:T(4,128)S(1)}, f32[4,4,64,128]{3,2,0,1:T(8,128)S(1)}) fusion(f32[4,4,69,138]{3,2,0,1:T(8,128)S(1)} %fusion.1, f32[4]{0:T(128)S(1)} %get-tuple-element.1270, f32[4]{0:T(128)S(1)} %get-tuple-element.1271, f32[4]{0:T(128)S(1)} %get-tuple-element.1272, f32[4]{0:T(128)S(1)} %get-tuple-element.1273, f32[4]{0:T(128)S(1)} %get-tuple-element.1274, ...), kind=kLoop, calls=%fused_computation.918 | loop fusion | flops 17432320 | bytes 35162144 | tf_op jit(solution)/shard_map/while/body/eval_jaxpr/cond/branch_1_fun/reduce_max | solution.py:82
  71.0 10.9 %conditional.9 = ((f32[4,64]{1,0:T(4,128)S(1)}, f32[4,64]{1,0:T(4,128)S(1)})) conditional(s32[]{:T(128)} %convert_element_type.73, (f32[4,64]{1,0:T(4,128)S(1)}, f32[4,64]{1,0:T(4,128)S(1)}) %tuple.400, (s32[]{:T(128)}, s32[]{:T(128)}, f32[4,6,11]{0,2,1:T(8,128)S(1)}, bf16[4,138,512]{2,1,0:T(8,128)(2,1)S(1)}, bf16[69,512]{1,0:T(8,128)(2,1)S(1)}, ...), branch_computations={%region_5.5_spmd, %region_6.8_spmd} | conditional | flops 57150952 | bytes 38340128 | solution.py:89
  72.5 9.2 %fusion.314 = (f32[4,64]{1,0:T(4,128)S(1)}, f32[4,4,64,128]{3,2,0,1:T(8,128)S(1)}) fusion(f32[4,4,69,138]{3,2,0,1:T(8,128)S(1)} %fusion.71, f32[4]{0:T(128)S(1)} %get-tuple-element.1336, f32[4]{0:T(128)S(1)} %get-tuple-element.1337, f32[4]{0:T(128)S(1)} %get-tuple-element.1338, f32[4]{0:T(128)S(1)} %get-tuple-element.1339, f32[4]{0:T(128)S(1)} %get-tuple-element.1340, ...), kind=kLoop, calls=%fused_computation.919 | loop fusion | flops 17432320 | bytes 35162144 | tf_op jit(solution)/shard_map/while/body/eval_jaxpr/cond/branch_1_fun/reduce_max | solution.py:82
  81.9 1.1 dynamic-slice_bitcast_fusion.6
  83.1 10.9 %conditional.9 = ((f32[4,64]{1,0:T(4,128)S(1)}, f32[4,64]{1,0:T(4,128)S(1)})) conditional(s32[]{:T(128)} %convert_element_type.73, (f32[4,64]{1,0:T(4,128)S(1)}, f32[4,64]{1,0:T(4,128)S(1)}) %tuple.400, (s32[]{:T(128)}, s32[]{:T(128)}, f32[4,6,11]{0,2,1:T(8,128)S(1)}, bf16[4,138,512]{2,1,0:T(8,128)(2,1)S(1)}, bf16[69,512]{1,0:T(8,128)(2,1)S(1)}, ...), branch_computations={%region_5.5_spmd, %region_6.8_spmd} | conditional | flops 57150952 | bytes 38340128 | solution.py:89
  84.5 9.2 %fusion.314 = (f32[4,64]{1,0:T(4,128)S(1)}, f32[4,4,64,128]{3,2,0,1:T(8,128)S(1)}) fusion(f32[4,4,69,138]{3,2,0,1:T(8,128)S(1)} %fusion.71, f32[4]{0:T(128)S(1)} %get-tuple-element.1336, f32[4]{0:T(128)S(1)} %get-tuple-element.1337, f32[4]{0:T(128)S(1)} %get-tuple-element.1338, f32[4]{0:T(128)S(1)} %get-tuple-element.1339, f32[4]{0:T(128)S(1)} %get-tuple-element.1340, ...), kind=kLoop, calls=%fused_computation.919 | loop fusion | flops 17432320 | bytes 35162144 | tf_op jit(solution)/shard_map/while/body/eval_jaxpr/cond/branch_1_fun/reduce_max | solution.py:82
  94.0 36.3 %while.47 = (s32[]{:T(128)}, f32[64,4,128]{2,0,1:T(8,128)S(1)}, f32[64,4,128]{2,0,1:T(8,128)S(1)}, s32[]{:T(128)}, bf16[2,4,138,512]{3,2,1,0:T(8,128)(2,1)}, /*i...) while((s32[]{:T(128)}, f32[64,4,128]{2,0,1:T(8,128)S(1)}, ...), condition=%wide.region_15.16_spmd, body=%wide.region_10.15_spmd.sunk | while | flops 183310304 | bytes 86701888 | solution.py:171
  94.2 1.2 dynamic-slice_bitcast_fusion.7
  95.7 11.1 %conditional.10 = (f32[64,4,128]{2,0,1:T(8,128)S(1)}) conditional(s32[]{:T(128)} %convert_element_type.74, f32[64,4,128]{2,0,1:T(8,128)S(1)} %get-tuple-element.1674, (f32[4,4]{1,0:T(4,128)S(1)}, s32[]{:T(128)}, s32[]{:T(128)}, f32[4,6,11]{0,2,1:T(8,128)S(1)}, bf16[4,138,512]{2,1,0:T(8,128)(2,1)S(1)}, /*index=5*/bf16[69,512]{1,0:T(8,128)(2,1)S(1)}, ...), branch_computations={%region_11.11_spmd, %region_12.12_spmd} | conditional | flops 91655144 | bytes 40164048 | solution.py:118
  97.1 9.0 %fusion.151 = f32[4,1,4,64,128]{4,3,0,2,1:T(8,128)S(1)} fusion(f32[4,4,69,138]{3,2,0,1:T(8,128)S(1)} %fusion.141, f32[4,64]{1,0:T(4,128)S(1)} %get-tuple-element.865, f32[4,64]{1,0:T(4,128)S(1)} %get-tuple-element.864, f32[4]{0:T(128)S(1)} %get-tuple-element.1134, f32[4]{0:T(128)S(1)} %get-tuple-element.1135, f32[4]{0:T(128)S(1)} %get-tuple-element.1136, ...), kind=kLoop, calls=%fused_computation.439 | loop fusion | flops 17563648 | bytes 35163168 | tf_op jit(solution)/shard_map/while/body/eval_jaxpr/cond/branch_1_fun/reshape | solution.py:105
  106.7 11.0 %conditional.11 = (f32[64,4,128]{2,0,1:T(8,128)S(1)}) conditional(s32[]{:T(128)} %convert_element_type.75, f32[64,4,128]{2,0,1:T(8,128)S(1)} %get-tuple-element.1675, (f32[4,4]{1,0:T(4,128)S(1)}, s32[]{:T(128)}, s32[]{:T(128)}, f32[4,6,11]{0,2,1:T(8,128)S(1)}, bf16[4,138,512]{2,1,0:T(8,128)(2,1)S(1)}, /*index=5*/bf16[69,512]{1,0:T(8,128)(2,1)S(1)}, ...), branch_computations={%region_13.13_spmd, %region_14.14_spmd} | conditional | flops 91655144 | bytes 40164048 | solution.py:118
  108.1 9.0 %fusion.236 = f32[4,1,4,64,128]{4,3,0,2,1:T(8,128)S(1)} fusion(f32[4,4,69,138]{3,2,0,1:T(8,128)S(1)} %fusion.226, f32[4,64]{1,0:T(4,128)S(1)} %get-tuple-element.875, f32[4,64]{1,0:T(4,128)S(1)} %get-tuple-element.874, f32[4]{0:T(128)S(1)} %get-tuple-element.1204, f32[4]{0:T(128)S(1)} %get-tuple-element.1205, f32[4]{0:T(128)S(1)} %get-tuple-element.1206, ...), kind=kLoop, calls=%fused_computation.674 | loop fusion | flops 17563648 | bytes 35163168 | tf_op jit(solution)/shard_map/while/body/eval_jaxpr/cond/branch_1_fun/reshape | solution.py:105
  117.8 1.2 dynamic-slice_bitcast_fusion.7
  119.3 11.0 %conditional.11 = (f32[64,4,128]{2,0,1:T(8,128)S(1)}) conditional(s32[]{:T(128)} %convert_element_type.75, f32[64,4,128]{2,0,1:T(8,128)S(1)} %get-tuple-element.1675, (f32[4,4]{1,0:T(4,128)S(1)}, s32[]{:T(128)}, s32[]{:T(128)}, f32[4,6,11]{0,2,1:T(8,128)S(1)}, bf16[4,138,512]{2,1,0:T(8,128)(2,1)S(1)}, /*index=5*/bf16[69,512]{1,0:T(8,128)(2,1)S(1)}, ...), branch_computations={%region_13.13_spmd, %region_14.14_spmd} | conditional | flops 91655144 | bytes 40164048 | solution.py:118
  120.7 9.0 %fusion.236 = f32[4,1,4,64,128]{4,3,0,2,1:T(8,128)S(1)} fusion(f32[4,4,69,138]{3,2,0,1:T(8,128)S(1)} %fusion.226, f32[4,64]{1,0:T(4,128)S(1)} %get-tuple-element.875, f32[4,64]{1,0:T(4,128)S(1)} %get-tuple-element.874, f32[4]{0:T(128)S(1)} %get-tuple-element.1204, f32[4]{0:T(128)S(1)} %get-tuple-element.1205, f32[4]{0:T(128)S(1)} %get-tuple-element.1206, ...), kind=kLoop, calls=%fused_computation.674 | loop fusion | flops 17563648 | bytes 35163168 | tf_op jit(solution)/shard_map/while/body/eval_jaxpr/cond/branch_1_fun/reshape | solution.py:105
  130.7 1.5 collective-permute-start.2
  132.2 2.8 %collective-permute-done.2 = bf16[64,512]{1,0:T(8,128)(2,1)S(1)} collective-permute-done((bf16[64,512]{1,0:T(8,128)(2,1)S(1)}, bf16[64,512]{1,0:T(8,128)(2,1)S(1)}, u32[]{:S(2)}, u32[]{:S(2)}) %collective-permute-start.2) | collective-permute-done | bytes 65568 | tf_op jit(solution)/shard_map/ppermute | solution.py:20
  135.0 10.3 %all_to_all.60 = bf16[4,32,512]{2,1,0:T(8,128)(2,1)S(1)} all-to-all(bf16[4,32,512]{2,1,0:T(8,128)(2,1)S(1)} %bitcast.665), channel_id=1, replica_groups=mesh['ctx'=8,'uly'=4] {'uly'}, dimensions={0} | all-to-all | bytes 262144 | tf_op jit(solution)/shard_map/all_to_all | solution.py:249
  (163 shorter events, 14.6 us)
Async XLA Ops:
  6.5 26.2 %copy-start.2 = (bf16[32,2048]{1,0:T(8,128)(2,1)S(1)}, bf16[32,2048]{1,0:T(8,128)(2,1)}, u32[]{:S(2)}) copy-start(bf16[32,2048]{1,0:T(8,128)(2,1)} %param.20) | copy-start | bytes 393220
  8.1 39.2 %copy-start.3 = (f32[4,6,11]{2,0,1:T(4,128)S(1)}, f32[4,6,11]{2,0,1:T(4,128)}, u32[]{:S(2)}) copy-start(f32[4,6,11]{2,0,1:T(4,128)} %param.21) | copy-start | bytes 3172
  8.1 12.5 %all-to-all-start.1 = ((bf16[4,32,512]{2,1,0:T(8,128)(2,1)}), bf16[4,32,512]{2,1,0:T(8,128)(2,1)S(1)}, u32[]{:S(2)}, u32[]{:S(2)}) async-start(bf16[4,32,512]{2,1,0:T(8,128)(2,1)} %pad_maximum_fusion), calls=%async_computation.1 | async-start | bytes 262144 | tf_op jit(solution)/shard_map/all_to_all | solution.py:185
  20.6 9.2 %all-to-all-start = ((bf16[32,4,512]{2,0,1:T(8,128)(2,1)}), bf16[32,4,512]{2,0,1:T(8,128)(2,1)S(1)}, u32[]{:S(2)}, u32[]{:S(2)}) async-start(bf16[32,4,512]{2,0,1:T(8,128)(2,1)} %bitcast.643), calls=%async_computation | async-start | bytes 262144 | tf_op jit(solution)/shard_map/all_to_all | solution.py:183
  23.9 35.1 %all-gather.7.cloned.1.call-start = ((), (), s32[]{:S(2)}) async-start(), calls=%async_computation.5 | async-start | bytes 1327104 | tf_op jit(solution)/shard_map/all_gather | solution.py:238
  29.8 2.1 %collective-permute-start = (bf16[15,512]{1,0:T(8,128)(2,1)S(1)}, bf16[15,512]{1,0:T(8,128)(2,1)S(1)}, u32[]{:S(2)}, u32[]{:S(2)}) collective-permute-start(bf16[15,512]{1,0:T(8,128)(2,1)S(1)} %pad_maximum_fusion.3), channel_id=1, source_target_pairs={{0,4},{4,8},{8,12},{12,16},{16,20},{20,24},{24,28},{1,5},{5,9},{9,... | collective-permute-start | bytes 46088 | tf_op jit(solution)/shard_map/ppermute | solution.py:16
  32.7 61.3 %all-gather.5.cloned.1.call-start = ((), (), s32[]{:S(2)}) async-start(), calls=%async_computation.4 | async-start | bytes 1179648 | tf_op jit(solution)/shard_map/all_gather | solution.py:239
  41.8 7.7 %collective-permute-start.1 = (bf16[69,512]{1,0:T(8,128)(2,1)S(1)}, bf16[69,512]{1,0:T(8,128)(2,1)S(1)}, u32[]{:S(2)}, u32[]{:S(2)}) collective-permute-start(bf16[69,512]{1,0:T(8,128)(2,1)S(1)} %get-tuple-element.1401), channel_id=1, source_target_pairs={{0,16},{4,20},{8,24},{12,28},{16,0},{20,4},{24,8},{28,12},{1,17},{... | collective-permute-start | bytes 211976 | tf_op jit(solution)/shard_map/ppermute | solution.py:20
  59.0 35.0 %copy-start.1 = (f32[4,4]{1,0:T(4,128)S(1)}, f32[4,4]{1,0:T(4,128)}, u32[]{:S(2)}) copy-start(f32[4,4]{1,0:T(4,128)} %param.22) | copy-start | bytes 196
  94.0 36.5 %copy-start.4 = (f32[512]{0:T(512)S(1)}, f32[512]{0:T(512)}, u32[]{:S(2)}) copy-start(f32[512]{0:T(512)} %param.23) | copy-start | bytes 6148
  94.2 1.4 copy-start
  117.8 1.4 copy-start
  130.7 4.3 %collective-permute-start.2 = (bf16[64,512]{1,0:T(8,128)(2,1)S(1)}, bf16[64,512]{1,0:T(8,128)(2,1)S(1)}, u32[]{:S(2)}, u32[]{:S(2)}) collective-permute-start(bf16[64,512]{1,0:T(8,128)(2,1)S(1)} %bitcast.671), channel_id=1, source_target_pairs={{0,16},{4,20},{8,24},{12,28},{16,0},{20,4},{24,8},{28,12},{1,17},{... | collective-permute-start | bytes 196616 | tf_op jit(solution)/shard_map/ppermute | solution.py:20
Sparse Core Ops, SparseCore 0:
  32.8 26.1 all-gather.6
  60.9 23.6 all-gather.4
